TPU v7x, 512 devices: a whole 4x4x16 slice. The times are simulated.
512 devices in a mesh: req: 128 (over x, z, core), mlp: 4 (over y).
Axes of the slice: x: 4, y: 4, z: 16, core: 2. Of those that a mesh axis runs over, the one named last changes fastest.
Arguments:
- queries: bfloat16 [32768, 8, 256], P('req', 'mlp'), may hold values from -7 to 7
- new_kv: bfloat16 [32768, 8, 512], P('req', 'mlp'), may hold values from -6 to 6
- cache_pool: bfloat16 [768, 128, 8, 512], P('req', None, 'mlp'), may hold values from -6 to 6
- page_table: int32 [128, 6], P('req'), may hold values from 0 to 5, each once within a row
- assignment: int32 [128], P('req'), may hold values from 0 to 127, each once
- lengths: int32 [128], replicated, may hold values from 1 to 768, 24576 in all
- lambda_vectors: float32 [4, 128], replicated, may hold values from -0.4 to 0.4
- subln_gain: float32 [256], replicated, may hold values from 0.5 to 1.5
- residual: bfloat16 [32768, 2048], P('req', 'mlp'), may hold values from -70 to 70
- out_weight: bfloat16 [2048, 2048], P('req', 'mlp'), may hold values from -0.125 to 0.125
- norm_gain: float32 [2048], replicated, may hold values from 0.5 to 1.5
- gate_weight: bfloat16 [2048, 3072], P('req', 'mlp'), may hold values from -0.125 to 0.125
- up_weight: bfloat16 [2048, 3072], P('req', 'mlp'), may hold values from -0.125 to 0.125
- down_weight_t: bfloat16 [2048, 3072], P('req', 'mlp'), may hold values from -0.109375 to 0.109375
Outputs:
- layer_out: bfloat16 [32768, 2048], P('req', 'mlp')
Inputs may be any that keep to these rules, and one draw needn't show every extreme that they name: `page_table`: row g lists the cache pages of slot g in logical order as offsets from page g * 6; each offset once in a row. `assignment`: every request is served by exactly one slot. `lengths`: indexed by request; some request has exactly 768 cached tokens.
All inputs are finite; a program needn't handle non-finite values.
Results may differ from a plain program's by a relative error of at most 0.011.
Values may be sent and summed in bfloat16 or wider, within the bound.
No kernel may reach another device: no remote copies, remote signals or barrier semaphores. Data moves between devices by JAX's collectives and lax.ppermute only.
A program may use at most 64 MiB of HBM per device.

v0:
```python
import jax
import jax.numpy as jnp
from jax import lax
from jax.sharding import Mesh, PartitionSpec as P

D = 2048
NEG_FILL = -1e30
LAMBDA_BASE = 0.2


def attend(
    queries, new_kv, cache_pool, page_table, assignment, lengths, lambda_vectors, subln_gain
):
    row_count, head_count, value_width = queries.shape
    half_size = value_width // 2
    score_scale = half_size ** (-0.5)
    request = assignment[0]
    cached = jnp.sum(
        jnp.where(jnp.arange(lengths.shape[0], dtype=jnp.int32) == request, lengths, 0)
    )
    pages = jnp.take(cache_pool, page_table[0], axis=0)
    cached_rows = pages.reshape(-1, head_count, cache_pool.shape[3])
    cache_len = cached_rows.shape[0]
    key_rows = jnp.concatenate([cached_rows, new_kv], axis=0)
    positions = jnp.arange(cache_len, dtype=jnp.int32)
    token_pos = jnp.arange(row_count, dtype=jnp.int32)
    visible = jnp.concatenate(
        [
            jnp.broadcast_to((positions < cached)[None, :], (row_count, cache_len)),
            token_pos[None, :] <= token_pos[:, None],
        ],
        axis=1,
    )
    value_rows = key_rows[:, :, 2 * half_size :]

    def one_map(query_rows, key_half):
        score = (
            jnp.einsum("nhd,khd->nhk", query_rows, key_half, preferred_element_type=jnp.float32)
            * score_scale
        )
        score = jnp.where(visible[:, None, :], score, NEG_FILL)
        row_max = jnp.max(score, axis=2, keepdims=True)
        exp_terms = jnp.where(visible[:, None, :], jnp.exp(score - row_max), 0.0)
        exp_total = jnp.sum(exp_terms, axis=2)
        mixed = jnp.einsum(
            "nhk,khd->nhd",
            exp_terms.astype(jnp.bfloat16),
            value_rows,
            preferred_element_type=jnp.float32,
        )
        return mixed / exp_total[:, :, None]

    map_one = one_map(queries[:, :, :half_size], key_rows[:, :, :half_size])
    map_two = one_map(queries[:, :, half_size:], key_rows[:, :, half_size : 2 * half_size])
    lambda_now = (
        jnp.exp(jnp.sum(lambda_vectors[0] * lambda_vectors[1]))
        - jnp.exp(jnp.sum(lambda_vectors[2] * lambda_vectors[3]))
        + LAMBDA_BASE
    )
    mix_out = map_one - lambda_now * map_two
    mix_out = (
        mix_out
        * lax.rsqrt(jnp.mean(mix_out * mix_out, axis=2, keepdims=True) + 1e-05)
        * subln_gain
        * (1.0 - LAMBDA_BASE)
    )
    return mix_out.astype(jnp.bfloat16).reshape(row_count, head_count * value_width)


def mlp_gather(block, axis_size):
    index = lax.axis_index("mlp")
    pieces = [block]
    for shift in range(1, axis_size):
        pieces.append(
            lax.ppermute(block, "mlp", [(i, (i + shift) % axis_size) for i in range(axis_size)])
        )
    stacked = jnp.stack(pieces, axis=0)
    source_of = (index - jnp.arange(axis_size, dtype=jnp.int32)) % axis_size
    gathered = jnp.take(stacked, source_of, axis=0)
    return jnp.concatenate([gathered[k] for k in range(axis_size)], axis=1)


def down_and_scatter(hidden_act, down_halves, axis_size, rows):
    index = lax.axis_index("mlp")
    nx, nz, nc = [lax.axis_size(name) for name in REQ_PARTS]
    n = hidden_act.shape[0]
    own = lax.axis_index("c")
    parts = []
    for half in down_halves:
        value = lax.dot_general(
            hidden_act, half, (((1,), (1,)), ((), ())), preferred_element_type=jnp.float32
        )
        parts.append(value.astype(jnp.bfloat16).reshape(n, nz, nx, rows))

    def block_for(target):
        picks = [lax.dynamic_index_in_dim(p, target, 2, keepdims=False) for p in parts]
        first = jnp.where(own == 0, picks[0], picks[1])
        second = jnp.where(own == 0, picks[1], picks[0])
        return jnp.stack([first, second], axis=2).reshape(n, -1)

    incoming = []
    for shift in range(1, axis_size):
        target = (index + shift) % axis_size
        incoming.append(
            lax.ppermute(
                block_for(target), "mlp", [(i, (i + shift) % axis_size) for i in range(axis_size)]
            )
        )
    total = block_for(index).astype(jnp.float32)
    for received in incoming:
        total = total + received.astype(jnp.float32)
    return total


REQ_PARTS = ("x", "z", "c")


def gather_over_xz(block):
    out = lax.all_gather(block, "x", axis=0, tiled=True)
    return lax.all_gather(out, "z", axis=0, tiled=True)


def swap_with_core(rows_xz):
    return [rows_xz, lax.ppermute(rows_xz, "c", [(0, 1), (1, 0)])]


def split_dot(act, halves):
    size = halves[0].shape[0]
    total = None
    for j, half in enumerate(halves):
        part = jnp.dot(act[:, j * size : (j + 1) * size], half, preferred_element_type=jnp.float32)
        total = part if total is None else total + part
    return total


def to_gathered_order(act, rows):
    nx, nz, nc = [lax.axis_size(name) for name in REQ_PARTS]
    n = act.shape[0]
    own = lax.axis_index("c")
    split = act.reshape(n, nx, nz, nc, rows)
    split = jnp.where(own == 0, split, split[:, :, :, ::-1, :])
    return split.transpose(0, 3, 2, 1, 4).reshape(n, -1)


def per_device(
    queries,
    new_kv,
    cache_pool,
    page_table,
    assignment,
    lengths,
    lambda_vectors,
    subln_gain,
    residual,
    out_weight,
    norm_gain,
    gate_weight,
    up_weight,
    down_weight_t,
):
    widths = [out_weight.shape[1], gate_weight.shape[1], up_weight.shape[1], down_weight_t.shape[1]]
    packed = jnp.concatenate([out_weight, gate_weight, up_weight, down_weight_t], axis=1)
    rows_xz = gather_over_xz(packed)
    attn_out = attend(
        queries, new_kv, cache_pool, page_table, assignment, lengths, lambda_vectors, subln_gain
    )
    mlp_size = D // residual.shape[1]
    heads_all = mlp_gather(attn_out, mlp_size)
    rows_xz, heads_all = lax.optimization_barrier((rows_xz, heads_all))
    halves = swap_with_core(rows_xz)
    bounds = [0]
    for w in widths:
        bounds.append(bounds[-1] + w)
    out_full, gate_full, up_full, down_full = [
        [half[:, bounds[i] : bounds[i + 1]] for half in halves] for i in range(4)
    ]
    rows = out_weight.shape[0]
    projected = split_dot(to_gathered_order(heads_all, rows), out_full)
    stream = (residual.astype(jnp.float32) + projected).astype(jnp.bfloat16)
    stream_all = mlp_gather(stream, mlp_size).astype(jnp.float32)
    squares = jnp.sum(stream_all * stream_all, axis=1, keepdims=True)
    normed = (stream_all * lax.rsqrt(squares / D + 1e-05) * norm_gain).astype(jnp.bfloat16)
    normed = to_gathered_order(normed, rows)
    gate_up = split_dot(normed, [half[:, bounds[1] : bounds[3]] for half in halves])
    gate_value = gate_up[:, : widths[1]]
    up_value = gate_up[:, widths[1] :]
    hidden_act = (jax.nn.silu(gate_value) * up_value).astype(jnp.bfloat16)
    summed = down_and_scatter(hidden_act, down_full, mlp_size, out_weight.shape[0])
    return (stream.astype(jnp.float32) + summed).astype(jnp.bfloat16)


def solution(mesh):
    split = Mesh(mesh.devices.reshape(4, 16, 2, mesh.devices.shape[1]), REQ_PARTS + ("mlp",))
    req = REQ_PARTS
    in_specs = (
        P(req, "mlp", None),
        P(req, "mlp", None),
        P(req, None, "mlp", None),
        P(req, None),
        P(req),
        P(),
        P(),
        P(),
        P(req, "mlp"),
        P(req, "mlp"),
        P(),
        P(req, "mlp"),
        P(req, "mlp"),
        P(req, "mlp"),
    )
    out_specs = P(req, "mlp")
    return jax.shard_map(
        per_device, mesh=split, in_specs=in_specs, out_specs=out_specs, check_vma=False
    )
```

profile of v0, /device:TPU:13, one launch (start us, length us, event | category | flops | bytes accessed | tf_op | source)
XLA Modules:
  0.0 189.5 jit_solution(5457327461825373114)
XLA Ops:
  6.5 0.9 pad_maximum_fusion.19
  7.4 9.8 %all_gather.6 = bf16[64,2816]{1,0:T(8,128)(2,1)} all-gather(bf16[16,2816]{1,0:T(8,128)(2,1)S(1)} %pad_maximum_fusion.19), channel_id=1, replica_groups=mesh['x'=4,'z'=16,'c'=2,'mlp'=4] {'x'}, dimensions={0}, use_global_device_ids=true | all-gather | bytes 450560 | tf_op jit(solution)/shard_map/all_gather | solution.py:119
  17.3 0.7 fusion.81
  17.9 5.6 %gather_fusion = bf16[6,128,2,512]{3,2,1,0:T(2,128)(2,1)} fusion(bf16[6,128,2,512]{3,2,1,0:T(2,128)(2,1)S(1)} %copy-done, s32[1024]{0:T(1024)S(1)} %pad_clamp_fusion.1), kind=kCustom, calls=%fused_computation.2 | custom fusion | bytes 3145752 | tf_op jit(solution)/shard_map/jit(_take)/gather | solution.py:21
  23.5 1.7 copy.47
  25.3 0.8 copy.48
  26.8 0.7 multiply_reduce_fusion.2
  28.8 0.7 fusion.79
  29.5 0.7 iota_compare_fusion.1
  30.4 0.2 pad_add_fusion
  30.6 1.8 fusion.110
  32.4 1.5 bitcast_select_fusion.4
  33.9 2.3 %fusion.111 = f32[256,2]{0,1:T(2,128)S(1)} fusion(pred[256,1024]{0,1:T(8,128)(4,1)S(1)} %pad_add_fusion, bf16[768,2,512]{2,0,1:T(8,128)(2,1)} %bitcast_select_fusion.4, bf16[256,2,512]{2,0,1:T(8,128)(2,1)} %copy.48, bf16[256,2,128]{2,1,0:T(2,128)(2,1)} %get-tuple-element.33), kind=kOutput, calls=%fused_computation.142 | convolution fusion | flops 137888768 | bytes 2754560 | tf_op jit(solution)/shard_map/sub | solution.py:43
  36.2 3.2 %fusion.21 = f32[256,2,256]{0,2,1:T(8,128)} fusion(f32[256,2]{0,1:T(2,128)S(1)} %fusion.111, pred[256,1024]{0,1:T(8,128)(4,1)S(1)} %pad_add_fusion, bf16[768,2,512]{2,0,1:T(8,128)(2,1)S(1)} %copy-done.1, bf16[256,2,512]{2,0,1:T(8,128)(2,1)} %copy.48, bf16[256,2,128]{2,1,0:T(2,128)(2,1)} %get-tuple-element.33), kind=kOutput, calls=%fused_computation.34 | convolution fusion | flops 408552960 | bytes 5376000 | tf_op jit(solution)/shard_map/nhk,khd->nhd/dot_general | solution.py:45
  39.4 2.0 %fusion.116 = f32[256,2]{0,1:T(2,128)S(1)} fusion(pred[256,1024]{0,1:T(8,128)(4,1)S(1)} %pad_add_fusion, bf16[256,2,512]{2,0,1:T(8,128)(2,1)} %copy.48, bf16[768,2,512]{2,0,1:T(8,128)(2,1)S(1)} %copy-done.1, bf16[256,2,128]{2,1,0:T(2,128)(2,1)S(1)} %get-tuple-element.32), kind=kOutput, calls=%fused_computation.143 | convolution fusion | flops 137888768 | bytes 2492416 | tf_op jit(solution)/shard_map/sub | solution.py:43
  41.4 3.5 %multiply_reduce_fusion.1 = (f32[256,2]{0,1:T(2,128)S(1)}, f32[256,2,256]{0,2,1:T(8,128)}) fusion(f32[256,2,256]{0,2,1:T(8,128)} %fusion.21, f32[256,2]{0,1:T(2,128)S(1)} %fusion.116, pred[256,1024]{0,1:T(8,128)(4,1)S(1)} %pad_add_fusion, bf16[256,2,512]{2,0,1:T(8,128)(2,1)} %copy.48, bf16[768,2,512]{2,0,1:T(8,128)(2,1)S(1)} %copy-done.1, ...), kind=kOutput, calls=%fused_computation.73 | convolution fusion | flops 409076736 | bytes 5902340 | tf_op jit(solution)/shard_map/nhk,khd->nhd/dot_general | solution.py:45
  44.9 1.2 multiply_convert_fusion.1
  46.0 3.2 %collective-permute-start = (bf16[256,512]{0,1:T(8,128)(2,1)S(1)}, bf16[256,512]{0,1:T(8,128)(2,1)S(1)}, u32[]{:S(2)}, u32[]{:S(2)}) collective-permute-start(bf16[256,512]{0,1:T(8,128)(2,1)S(1)} %bitcast.105), channel_id=1, source_target_pairs={{0,1},{1,2},{2,3},{3,0},{4,5},{5,6},{6,7},{7,4},{8,9},{9,10},{10,1... | collective-permute-start | bytes 786440 | tf_op jit(solution)/shard_map/ppermute | solution.py:75
  49.2 2.6 %collective-permute-start.1 = (bf16[256,512]{0,1:T(8,128)(2,1)S(1)}, bf16[256,512]{0,1:T(8,128)(2,1)S(1)}, u32[]{:S(2)}, u32[]{:S(2)}) collective-permute-start(bf16[256,512]{0,1:T(8,128)(2,1)S(1)} %bitcast.106), channel_id=1, source_target_pairs={{0,2},{1,3},{2,0},{3,1},{4,6},{5,7},{6,4},{7,5},{8,10},{9,11},{10,... | collective-permute-start | bytes 786440 | tf_op jit(solution)/shard_map/ppermute | solution.py:75
  51.8 4.0 %collective-permute-start.2 = (bf16[256,512]{0,1:T(8,128)(2,1)S(1)}, bf16[256,512]{0,1:T(8,128)(2,1)S(1)}, u32[]{:S(2)}, u32[]{:S(2)}) collective-permute-start(bf16[256,512]{0,1:T(8,128)(2,1)S(1)} %bitcast.107), channel_id=1, source_target_pairs={{0,3},{1,0},{2,1},{3,2},{4,7},{5,4},{6,5},{7,6},{8,11},{9,8},{10,9... | collective-permute-start | bytes 786440 | tf_op jit(solution)/shard_map/ppermute | solution.py:75
  55.9 2.4 %collective-permute-done.1 = bf16[256,512]{0,1:T(8,128)(2,1)S(1)} collective-permute-done((bf16[256,512]{0,1:T(8,128)(2,1)S(1)}, bf16[256,512]{0,1:T(8,128)(2,1)S(1)}, u32[]{:S(2)}, u32[]{:S(2)}) %collective-permute-start.1) | collective-permute-done | bytes 262176 | tf_op jit(solution)/shard_map/ppermute | solution.py:75
  58.3 2.8 %collective-permute-done.2 = bf16[256,512]{0,1:T(8,128)(2,1)S(1)} collective-permute-done((bf16[256,512]{0,1:T(8,128)(2,1)S(1)}, bf16[256,512]{0,1:T(8,128)(2,1)S(1)}, u32[]{:S(2)}, u32[]{:S(2)}) %collective-permute-start.2) | collective-permute-done | bytes 262176 | tf_op jit(solution)/shard_map/ppermute | solution.py:75
  61.0 1.1 pad_maximum_fusion
  62.2 1.9 gather_fusion.1
  64.0 0.2 broadcast_select_fusion.1
  64.4 39.7 %all-gather.2.cloned.1.call-done = bf16[1024,2816]{1,0:T(8,128)(2,1)} async-done(((bf16[64,2816]{1,0:T(8,128)(2,1)}), bf16[1024,2816]{1,0:T(8,128)(2,1)}) %all-gather.2.cloned.1.call-update) | async-done | bytes 5767184 | tf_op jit(solution)/shard_map/all_gather | solution.py:120
  104.0 7.7 %collective-permute-start.3 = (bf16[1024,2816]{1,0:T(8,128)(2,1)}, bf16[1024,2816]{1,0:T(8,128)(2,1)}, u32[]{:S(2)}, u32[]{:S(2)}) collective-permute-start(bf16[1024,2816]{1,0:T(8,128)(2,1)} %all-gather.2.cloned.1.call-done), channel_id=1, source_target_pairs={{0,4},{4,0},{1,5},{5,1},{2,6},{6,2},{3,7},{7,3},{8,12},{12,8},{9,1... | collective-permute-start | bytes 17301512 | tf_op jit(solution)/shard_map/ppermute | solution.py:124
  111.8 0.4 fusion.27
  112.4 1.7 fusion.31
  114.1 7.0 %collective-permute-done.3 = bf16[1024,2816]{1,0:T(8,128)(2,1)} collective-permute-done((bf16[1024,2816]{1,0:T(8,128)(2,1)}, bf16[1024,2816]{1,0:T(8,128)(2,1)}, u32[]{:S(2)}, u32[]{:S(2)}) %collective-permute-start.3) | collective-permute-done | bytes 5767200 | tf_op jit(solution)/shard_map/ppermute | solution.py:124
  121.1 1.7 fusion.26
  122.8 3.1 %collective-permute-start.4 = (bf16[256,512]{1,0:T(8,128)(2,1)S(1)}, bf16[256,512]{1,0:T(8,128)(2,1)S(1)}, u32[]{:S(2)}, u32[]{:S(2)}) collective-permute-start(bf16[256,512]{1,0:T(8,128)(2,1)S(1)} %fusion.26), channel_id=1, source_target_pairs={{0,1},{1,2},{2,3},{3,0},{4,5},{5,6},{6,7},{7,4},{8,9},{9,10},{10,1... | collective-permute-start | bytes 786440 | tf_op jit(solution)/shard_map/ppermute | solution.py:75
  125.9 2.6 %collective-permute-start.5 = (bf16[256,512]{1,0:T(8,128)(2,1)S(1)}, bf16[256,512]{1,0:T(8,128)(2,1)S(1)}, u32[]{:S(2)}, u32[]{:S(2)}) collective-permute-start(bf16[256,512]{1,0:T(8,128)(2,1)S(1)} %fusion.26), channel_id=1, source_target_pairs={{0,2},{1,3},{2,0},{3,1},{4,6},{5,7},{6,4},{7,5},{8,10},{9,11},{10,... | collective-permute-start | bytes 786440 | tf_op jit(solution)/shard_map/ppermute | solution.py:75
  128.5 4.1 %collective-permute-start.6 = (bf16[256,512]{1,0:T(8,128)(2,1)S(1)}, bf16[256,512]{1,0:T(8,128)(2,1)S(1)}, u32[]{:S(2)}, u32[]{:S(2)}) collective-permute-start(bf16[256,512]{1,0:T(8,128)(2,1)S(1)} %fusion.26), channel_id=1, source_target_pairs={{0,3},{1,0},{2,1},{3,2},{4,7},{5,4},{6,5},{7,6},{8,11},{9,8},{10,9... | collective-permute-start | bytes 786440 | tf_op jit(solution)/shard_map/ppermute | solution.py:75
  132.8 3.8 %collective-permute-done.5 = bf16[256,512]{1,0:T(8,128)(2,1)S(1)} collective-permute-done((bf16[256,512]{1,0:T(8,128)(2,1)S(1)}, bf16[256,512]{1,0:T(8,128)(2,1)S(1)}, u32[]{:S(2)}, u32[]{:S(2)}) %collective-permute-start.5) | collective-permute-done | bytes 262176 | tf_op jit(solution)/shard_map/ppermute | solution.py:75
  136.5 6.6 %collective-permute-done.6 = bf16[256,512]{1,0:T(8,128)(2,1)S(1)} collective-permute-done((bf16[256,512]{1,0:T(8,128)(2,1)S(1)}, bf16[256,512]{1,0:T(8,128)(2,1)S(1)}, u32[]{:S(2)}, u32[]{:S(2)}) %collective-permute-start.6) | collective-permute-done | bytes 262176 | tf_op jit(solution)/shard_map/ppermute | solution.py:75
  143.1 1.1 pad_maximum_fusion.2
  144.3 1.8 gather_fusion.2
  146.1 0.2 broadcast_select_fusion
  146.3 0.1 slice_bitcast_fusion.7
  146.4 0.3 multiply_reduce_fusion
  146.7 0.1 copy.56
  146.9 0.1 copy.57
  147.0 0.1 copy.58
  147.3 0.3 multiply_convert_fusion
  147.6 0.5 fusion.28
  148.2 2.9 %fusion.4 = f32[256,1536]{1,0:T(8,128)S(1)} fusion(bf16[1024,2816]{1,0:T(8,128)(2,1)} %all-gather.2.cloned.1.call-done, bf16[256,2048]{0,1:T(8,128)(2,1)S(1)} %bitcast.95), kind=kOutput, calls=%fused_computation.7 | convolution fusion | flops 805306368 | bytes 5242880 | tf_op jit(solution)/shard_map/dot_general | solution.py:131
  151.1 2.9 %fusion.6 = f32[256,1536]{1,0:T(8,128)S(1)} fusion(f32[256,1536]{1,0:T(8,128)S(1)} %fusion.4, bf16[1024,2816]{1,0:T(8,128)(2,1)} %collective-permute-done.3, bf16[256,2048]{0,1:T(8,128)(2,1)S(1)} %bitcast.96), kind=kOutput, calls=%fused_computation.9 | convolution fusion | flops 805699584 | bytes 6815744 | tf_op jit(solution)/shard_map/dot_general | solution.py:131
  154.0 0.2 fusion.41
  154.3 0.7 copy-done.3
  155.0 2.0 %fusion.15 = bf16[256,1024]{1,0:T(8,128)(2,1)S(1)} fusion(bf16[256,768]{1,0:T(8,128)(2,1)S(1)} %fusion.41, bf16[1024,2816]{1,0:T(8,128)(2,1)} %all-gather.2.cloned.1.call-done), kind=kOutput, calls=%fused_computation.29 | convolution fusion | flops 402915328 | bytes 2490368 | tf_op jit(solution)/shard_map/dot_general | solution.py:90
  157.0 0.2 copy.61
  157.2 2.1 %fusion.18 = bf16[256,1024]{1,0:T(8,128)(2,1)S(1)} fusion(bf16[256,768]{1,0:T(8,128)(2,1)} %copy-done.3, bf16[1024,2816]{1,0:T(8,128)(2,1)} %collective-permute-done.3), kind=kOutput, calls=%fused_computation.30 | convolution fusion | flops 402915328 | bytes 2490368 | tf_op jit(solution)/shard_map/dot_general | solution.py:90
  159.4 0.2 copy.62
  159.7 0.8 copy.63
  160.6 1.9 %collective-permute-start.7 = (bf16[256,512]{1,0:T(8,128)(2,1)}, bf16[256,512]{1,0:T(8,128)(2,1)}, u32[]{:S(2)}, u32[]{:S(2)}) collective-permute-start(bf16[256,512]{1,0:T(8,128)(2,1)} %copy.63), channel_id=1, source_target_pairs={{0,1},{1,2},{2,3},{3,0},{4,5},{5,6},{6,7},{7,4},{8,9},{9,10},{10,1... | collective-permute-start | bytes 786440 | tf_op jit(solution)/shard_map/ppermute | solution.py:105
  162.6 0.8 copy.65
  163.4 2.2 %collective-permute-start.8 = (bf16[256,512]{1,0:T(8,128)(2,1)}, bf16[256,512]{1,0:T(8,128)(2,1)S(1)}, u32[]{:S(2)}, u32[]{:S(2)}) collective-permute-start(bf16[256,512]{1,0:T(8,128)(2,1)} %copy.65), channel_id=1, source_target_pairs={{0,2},{1,3},{2,0},{3,1},{4,6},{5,7},{6,4},{7,5},{8,10},{9,11},{10,... | collective-permute-start | bytes 786440 | tf_op jit(solution)/shard_map/ppermute | solution.py:105
  165.6 0.8 copy.66
  166.4 4.0 %collective-permute-start.9 = (bf16[256,512]{1,0:T(8,128)(2,1)}, bf16[256,512]{1,0:T(8,128)(2,1)S(1)}, u32[]{:S(2)}, u32[]{:S(2)}) collective-permute-start(bf16[256,512]{1,0:T(8,128)(2,1)} %copy.66), channel_id=1, source_target_pairs={{0,3},{1,0},{2,1},{3,2},{4,7},{5,4},{6,5},{7,6},{8,11},{9,8},{10,9... | collective-permute-start | bytes 786440 | tf_op jit(solution)/shard_map/ppermute | solution.py:105
  170.5 0.2 copy.64
  170.7 3.0 %collective-permute-done.8 = bf16[256,512]{1,0:T(8,128)(2,1)S(1)} collective-permute-done((bf16[256,512]{1,0:T(8,128)(2,1)}, bf16[256,512]{1,0:T(8,128)(2,1)S(1)}, u32[]{:S(2)}, u32[]{:S(2)}) %collective-permute-start.8) | collective-permute-done | bytes 262176 | tf_op jit(solution)/shard_map/ppermute | solution.py:105
  173.7 7.1 %collective-permute-done.9 = bf16[256,512]{1,0:T(8,128)(2,1)S(1)} collective-permute-done((bf16[256,512]{1,0:T(8,128)(2,1)}, bf16[256,512]{1,0:T(8,128)(2,1)S(1)}, u32[]{:S(2)}, u32[]{:S(2)}) %collective-permute-start.9) | collective-permute-done | bytes 262176 | tf_op jit(solution)/shard_map/ppermute | solution.py:105
  180.8 1.8 add_convert_fusion
  (44 shorter events, 1.1 us)
Async XLA Ops:
  6.5 11.4 %copy-start = (bf16[6,128,2,512]{3,2,1,0:T(2,128)(2,1)S(1)}, bf16[6,128,2,512]{3,2,1,0:T(2,128)(2,1)}, u32[]{:S(2)}) copy-start(bf16[6,128,2,512]{3,2,1,0:T(2,128)(2,1)} %param.18) | copy-start | bytes 4718596
  6.5 97.5 %all-gather.2.cloned.1.call-start = ((), (), s32[]{:S(2)}) async-start(), calls=%async_computation | async-start | bytes 6127616 | tf_op jit(solution)/shard_map/all_gather | solution.py:120
  23.5 1.8 copy-start.2
  23.5 3.3 %copy-start.5 = (f32[4,128]{1,0:T(4,128)S(1)}, f32[4,128]{1,0:T(4,128)}, u32[]{:S(2)}) copy-start(f32[4,128]{1,0:T(4,128)} %param.22) | copy-start | bytes 6148
  23.5 5.3 %copy-start.8 = (s32[128]{0:T(128)S(1)}, s32[128]{0:T(128)}, u32[]{:S(2)}) copy-start(s32[128]{0:T(128)} %param.21) | copy-start | bytes 1540
  23.5 6.8 %copy-start.9 = (s32[1,6]{1,0:T(1,128)S(1)}, s32[1,6]{1,0:T(1,128)}, u32[]{:S(2)}) copy-start(s32[1,6]{1,0:T(1,128)} %param.19) | copy-start | bytes 76
  33.9 2.3 %copy-start.1 = (bf16[768,2,512]{2,0,1:T(8,128)(2,1)S(1)}, bf16[768,2,512]{2,0,1:T(8,128)(2,1)}, u32[]{:S(2)}) copy-start(bf16[768,2,512]{2,0,1:T(8,128)(2,1)} %bitcast_select_fusion.4) | copy-start | bytes 4718596
  41.4 3.5 %copy-start.6 = (f32[256]{0:T(256)S(1)}, f32[256]{0:T(256)}, u32[]{:S(2)}) copy-start(f32[256]{0:T(256)} %param.23) | copy-start | bytes 3076
  46.0 9.8 %collective-permute-start = (bf16[256,512]{0,1:T(8,128)(2,1)S(1)}, bf16[256,512]{0,1:T(8,128)(2,1)S(1)}, u32[]{:S(2)}, u32[]{:S(2)}) collective-permute-start(bf16[256,512]{0,1:T(8,128)(2,1)S(1)} %bitcast.105), channel_id=1, source_target_pairs={{0,1},{1,2},{2,3},{3,0},{4,5},{5,6},{6,7},{7,4},{8,9},{9,10},{10,1... | collective-permute-start | bytes 786440 | tf_op jit(solution)/shard_map/ppermute | solution.py:75
  49.2 9.0 %collective-permute-start.1 = (bf16[256,512]{0,1:T(8,128)(2,1)S(1)}, bf16[256,512]{0,1:T(8,128)(2,1)S(1)}, u32[]{:S(2)}, u32[]{:S(2)}) collective-permute-start(bf16[256,512]{0,1:T(8,128)(2,1)S(1)} %bitcast.106), channel_id=1, source_target_pairs={{0,2},{1,3},{2,0},{3,1},{4,6},{5,7},{6,4},{7,5},{8,10},{9,11},{10,... | collective-permute-start | bytes 786440 | tf_op jit(solution)/shard_map/ppermute | solution.py:75
  51.8 9.2 %collective-permute-start.2 = (bf16[256,512]{0,1:T(8,128)(2,1)S(1)}, bf16[256,512]{0,1:T(8,128)(2,1)S(1)}, u32[]{:S(2)}, u32[]{:S(2)}) collective-permute-start(bf16[256,512]{0,1:T(8,128)(2,1)S(1)} %bitcast.107), channel_id=1, source_target_pairs={{0,3},{1,0},{2,1},{3,2},{4,7},{5,4},{6,5},{7,6},{8,11},{9,8},{10,9... | collective-permute-start | bytes 786440 | tf_op jit(solution)/shard_map/ppermute | solution.py:75
  104.0 17.1 %collective-permute-start.3 = (bf16[1024,2816]{1,0:T(8,128)(2,1)}, bf16[1024,2816]{1,0:T(8,128)(2,1)}, u32[]{:S(2)}, u32[]{:S(2)}) collective-permute-start(bf16[1024,2816]{1,0:T(8,128)(2,1)} %all-gather.2.cloned.1.call-done), channel_id=1, source_target_pairs={{0,4},{4,0},{1,5},{5,1},{2,6},{6,2},{3,7},{7,3},{8,12},{12,8},{9,1... | collective-permute-start | bytes 17301512 | tf_op jit(solution)/shard_map/ppermute | solution.py:124
  112.2 8.9 %copy-start.7 = (bf16[256,512]{1,0:T(8,128)(2,1)S(1)}, bf16[256,512]{1,0:T(8,128)(2,1)}, u32[]{:S(2)}) copy-start(bf16[256,512]{1,0:T(8,128)(2,1)} %param.24) | copy-start | bytes 786436
  114.1 18.5 %copy-start.4 = (f32[2048]{0:T(1024)S(1)}, f32[2048]{0:T(1024)}, u32[]{:S(2)}) copy-start(f32[2048]{0:T(1024)} %param.26) | copy-start | bytes 24580
  122.8 9.9 %collective-permute-start.4 = (bf16[256,512]{1,0:T(8,128)(2,1)S(1)}, bf16[256,512]{1,0:T(8,128)(2,1)S(1)}, u32[]{:S(2)}, u32[]{:S(2)}) collective-permute-start(bf16[256,512]{1,0:T(8,128)(2,1)S(1)} %fusion.26), channel_id=1, source_target_pairs={{0,1},{1,2},{2,3},{3,0},{4,5},{5,6},{6,7},{7,4},{8,9},{9,10},{10,1... | collective-permute-start | bytes 786440 | tf_op jit(solution)/shard_map/ppermute | solution.py:75
  125.9 10.6 %collective-permute-start.5 = (bf16[256,512]{1,0:T(8,128)(2,1)S(1)}, bf16[256,512]{1,0:T(8,128)(2,1)S(1)}, u32[]{:S(2)}, u32[]{:S(2)}) collective-permute-start(bf16[256,512]{1,0:T(8,128)(2,1)S(1)} %fusion.26), channel_id=1, source_target_pairs={{0,2},{1,3},{2,0},{3,1},{4,6},{5,7},{6,4},{7,5},{8,10},{9,11},{10,... | collective-permute-start | bytes 786440 | tf_op jit(solution)/shard_map/ppermute | solution.py:75
  128.5 14.7 %collective-permute-start.6 = (bf16[256,512]{1,0:T(8,128)(2,1)S(1)}, bf16[256,512]{1,0:T(8,128)(2,1)S(1)}, u32[]{:S(2)}, u32[]{:S(2)}) collective-permute-start(bf16[256,512]{1,0:T(8,128)(2,1)S(1)} %fusion.26), channel_id=1, source_target_pairs={{0,3},{1,0},{2,1},{3,2},{4,7},{5,4},{6,5},{7,6},{8,11},{9,8},{10,9... | collective-permute-start | bytes 786440 | tf_op jit(solution)/shard_map/ppermute | solution.py:75
  154.2 0.8 copy-start.3
  160.6 10.1 %collective-permute-start.7 = (bf16[256,512]{1,0:T(8,128)(2,1)}, bf16[256,512]{1,0:T(8,128)(2,1)}, u32[]{:S(2)}, u32[]{:S(2)}) collective-permute-start(bf16[256,512]{1,0:T(8,128)(2,1)} %copy.63), channel_id=1, source_target_pairs={{0,1},{1,2},{2,3},{3,0},{4,5},{5,6},{6,7},{7,4},{8,9},{9,10},{10,1... | collective-permute-start | bytes 786440 | tf_op jit(solution)/shard_map/ppermute | solution.py:105
  163.4 10.3 %collective-permute-start.8 = (bf16[256,512]{1,0:T(8,128)(2,1)}, bf16[256,512]{1,0:T(8,128)(2,1)S(1)}, u32[]{:S(2)}, u32[]{:S(2)}) collective-permute-start(bf16[256,512]{1,0:T(8,128)(2,1)} %copy.65), channel_id=1, source_target_pairs={{0,2},{1,3},{2,0},{3,1},{4,6},{5,7},{6,4},{7,5},{8,10},{9,11},{10,... | collective-permute-start | bytes 786440 | tf_op jit(solution)/shard_map/ppermute | solution.py:105
  166.4 14.4 %collective-permute-start.9 = (bf16[256,512]{1,0:T(8,128)(2,1)}, bf16[256,512]{1,0:T(8,128)(2,1)S(1)}, u32[]{:S(2)}, u32[]{:S(2)}) collective-permute-start(bf16[256,512]{1,0:T(8,128)(2,1)} %copy.66), channel_id=1, source_target_pairs={{0,3},{1,0},{2,1},{3,2},{4,7},{5,4},{6,5},{7,6},{8,11},{9,8},{10,9... | collective-permute-start | bytes 786440 | tf_op jit(solution)/shard_map/ppermute | solution.py:105
Sparse Core Ops, SparseCore 0:
  17.4 86.6 all-gather.1
where the time goes:
time: 190 us
  waiting for transfers between devices  72.5 us (38%)
  starting transfers between devices  35.2 us (19%)
  matrix products  24.2 us (13%)
  local copies, waits for them, and re-layouts  18.8 us (10%)
  between operations  15.9 us (8%)
  other arithmetic  13 us (7%)
  blocking collectives  9.79 us (5%)
    all_gather x1, waiting for transfers between devices, gather_over_xz(): return lax.all_gather(out, 'z', axis=0, tiled=True)  39.7 us
    ppermute x6, starting transfers between devices, mlp_gather(): lax.ppermute(block, 'mlp', [(i, (i + shift) % axis_size) for i in range(a...  19.5 us
    ppermute x6, waiting for transfers between devices, mlp_gather(): lax.ppermute(block, 'mlp', [(i, (i + shift) % axis_size) for i in range(a...  15.6 us
    ppermute x3, waiting for transfers between devices, down_and_scatter(): lax.ppermute(block_for(target), 'mlp', [(i, (i + shift) % axis_size) for...  10.2 us
    all_gather x1, blocking collectives, gather_over_xz(): out = lax.all_gather(block, 'x', axis=0, tiled=True)  9.79 us
    dot_general x4, matrix products, split_dot(): jnp.dot(act[:, j * size:(j + 1) * size], half, preferred_element_type=jnp...  9.13 us
    ppermute x3, starting transfers between devices, down_and_scatter(): lax.ppermute(block_for(target), 'mlp', [(i, (i + shift) % axis_size) for...  8.04 us
    ppermute x1, starting transfers between devices, swap_with_core(): return [rows_xz, lax.ppermute(rows_xz, 'c', [(0, 1), (1, 0)])]  7.73 us
  transfers between devices with their start and end apart: 11, of which 8 were waited for; matrix products, arithmetic and copies ran while one was open for 18% of the time, Pallas kernels for 0%

commit v1 on v0

--- a/solution.py
+++ b/solution.py
@@ -116,7 +116,9 @@
 
 
 def gather_over_xz(block):
-    out = lax.all_gather(block, "x", axis=0, tiled=True)
+    out = jnp.concatenate(
+        lax.all_to_all(jnp.stack([block] * lax.axis_size("x")), "x", 0, 0), axis=0
+    )
     return lax.all_gather(out, "z", axis=0, tiled=True)
 
 

time: 190 us -> 187 us (0.984)
  the two profiles are of different devices: /device:TPU:13 before, /device:TPU:15 now
where the time goes in v1:
time: 187 us; the launch traced here: 186 us
  waiting for transfers between devices  69.9 us (37%)
  starting transfers between devices  35.3 us (19%)
  matrix products  24.1 us (13%)
  local copies, waits for them, and re-layouts  18.8 us (10%)
  between operations  15.9 us (9%)
  other arithmetic  13 us (7%)
  blocking collectives  9.14 us (5%)
    all_gather x1, waiting for transfers between devices, gather_over_xz(): return lax.all_gather(out, 'z', axis=0, tiled=True)  35.2 us
    ppermute x6, starting transfers between devices, mlp_gather(): lax.ppermute(block, 'mlp', [(i, (i + shift) % axis_size) for i in range(a...  19.2 us
    ppermute x6, waiting for transfers between devices, mlp_gather(): lax.ppermute(block, 'mlp', [(i, (i + shift) % axis_size) for i in range(a...  17.8 us
    ppermute x3, waiting for transfers between devices, down_and_scatter(): lax.ppermute(block_for(target), 'mlp', [(i, (i + shift) % axis_size) for...  9.85 us
    all_to_all x1, blocking collectives, gather_over_xz(): lax.all_to_all(jnp.stack([block] * lax.axis_size('x')), 'x', 0, 0)  9.14 us
    dot_general x4, matrix products, split_dot(): jnp.dot(act[:, j * size:(j + 1) * size], half, preferred_element_type=jnp...  9.13 us
    ppermute x3, starting transfers between devices, down_and_scatter(): lax.ppermute(block_for(target), 'mlp', [(i, (i + shift) % axis_size) for...  8.36 us
    ppermute x1, starting transfers between devices, swap_with_core(): return [rows_xz, lax.ppermute(rows_xz, 'c', [(0, 1), (1, 0)])]  7.73 us
  transfers between devices with their start and end apart: 11, of which 8 were waited for; matrix products, arithmetic and copies ran while one was open for 18% of the time, Pallas kernels for 0%

profile of v1, /device:TPU:15, one launch (start us, length us, event | category | flops | bytes accessed | tf_op | source)
XLA Modules:
  0.0 186.3 jit_solution(17714329373888779499)
XLA Ops:
  6.5 0.9 pad_maximum_fusion.19
  7.5 9.1 %all_to_all.5 = bf16[4,16,2816]{2,1,0:T(8,128)(2,1)} all-to-all(bf16[4,16,2816]{2,1,0:T(8,128)(2,1)S(1)} %stack.54), channel_id=1, replica_groups=mesh['x'=4,'z'=16,'c'=2,'mlp'=4] {'x'}, dimensions={0} | all-to-all | bytes 720896 | tf_op jit(solution)/shard_map/all_to_all | solution.py:120
  16.6 0.7 fusion.81
  17.3 5.6 %gather_fusion = bf16[6,128,2,512]{3,2,1,0:T(2,128)(2,1)} fusion(bf16[6,128,2,512]{3,2,1,0:T(2,128)(2,1)S(1)} %copy-done, s32[1024]{0:T(1024)S(1)} %pad_clamp_fusion.1), kind=kCustom, calls=%fused_computation.2 | custom fusion | bytes 3145752 | tf_op jit(solution)/shard_map/jit(_take)/gather | solution.py:21
  22.9 1.7 copy.47
  24.7 0.8 copy.48
  26.2 0.7 multiply_reduce_fusion.2
  28.2 0.7 fusion.79
  28.9 0.7 iota_compare_fusion.1
  29.8 0.2 pad_add_fusion
  30.0 1.8 fusion.110
  31.8 1.5 bitcast_select_fusion.4
  33.3 2.3 %fusion.111 = f32[256,2]{0,1:T(2,128)S(1)} fusion(pred[256,1024]{0,1:T(8,128)(4,1)S(1)} %pad_add_fusion, bf16[768,2,512]{2,0,1:T(8,128)(2,1)} %bitcast_select_fusion.4, bf16[256,2,512]{2,0,1:T(8,128)(2,1)} %copy.48, bf16[256,2,128]{2,1,0:T(2,128)(2,1)} %get-tuple-element.33), kind=kOutput, calls=%fused_computation.142 | convolution fusion | flops 137888768 | bytes 2754560 | tf_op jit(solution)/shard_map/sub | solution.py:43
  35.5 3.2 %fusion.21 = f32[256,2,256]{0,2,1:T(8,128)} fusion(f32[256,2]{0,1:T(2,128)S(1)} %fusion.111, pred[256,1024]{0,1:T(8,128)(4,1)S(1)} %pad_add_fusion, bf16[768,2,512]{2,0,1:T(8,128)(2,1)S(1)} %copy-done.1, bf16[256,2,512]{2,0,1:T(8,128)(2,1)} %copy.48, bf16[256,2,128]{2,1,0:T(2,128)(2,1)} %get-tuple-element.33), kind=kOutput, calls=%fused_computation.34 | convolution fusion | flops 408552960 | bytes 5376000 | tf_op jit(solution)/shard_map/nhk,khd->nhd/dot_general | solution.py:45
  38.8 2.0 %fusion.116 = f32[256,2]{0,1:T(2,128)S(1)} fusion(pred[256,1024]{0,1:T(8,128)(4,1)S(1)} %pad_add_fusion, bf16[256,2,512]{2,0,1:T(8,128)(2,1)} %copy.48, bf16[768,2,512]{2,0,1:T(8,128)(2,1)S(1)} %copy-done.1, bf16[256,2,128]{2,1,0:T(2,128)(2,1)S(1)} %get-tuple-element.32), kind=kOutput, calls=%fused_computation.143 | convolution fusion | flops 137888768 | bytes 2492416 | tf_op jit(solution)/shard_map/sub | solution.py:43
  40.8 3.4 %multiply_reduce_fusion.1 = (f32[256,2]{0,1:T(2,128)S(1)}, f32[256,2,256]{0,2,1:T(8,128)}) fusion(f32[256,2,256]{0,2,1:T(8,128)} %fusion.21, f32[256,2]{0,1:T(2,128)S(1)} %fusion.116, pred[256,1024]{0,1:T(8,128)(4,1)S(1)} %pad_add_fusion, bf16[256,2,512]{2,0,1:T(8,128)(2,1)} %copy.48, bf16[768,2,512]{2,0,1:T(8,128)(2,1)S(1)} %copy-done.1, ...), kind=kOutput, calls=%fused_computation.73 | convolution fusion | flops 409076736 | bytes 5902340 | tf_op jit(solution)/shard_map/nhk,khd->nhd/dot_general | solution.py:45
  44.1 1.2 multiply_convert_fusion.1
  45.3 3.2 %collective-permute-start = (bf16[256,512]{0,1:T(8,128)(2,1)S(1)}, bf16[256,512]{0,1:T(8,128)(2,1)S(1)}, u32[]{:S(2)}, u32[]{:S(2)}) collective-permute-start(bf16[256,512]{0,1:T(8,128)(2,1)S(1)} %bitcast.107), channel_id=1, source_target_pairs={{0,1},{1,2},{2,3},{3,0},{4,5},{5,6},{6,7},{7,4},{8,9},{9,10},{10,1... | collective-permute-start | bytes 786440 | tf_op jit(solution)/shard_map/ppermute | solution.py:75
  48.5 2.6 %collective-permute-start.1 = (bf16[256,512]{0,1:T(8,128)(2,1)S(1)}, bf16[256,512]{0,1:T(8,128)(2,1)S(1)}, u32[]{:S(2)}, u32[]{:S(2)}) collective-permute-start(bf16[256,512]{0,1:T(8,128)(2,1)S(1)} %bitcast.108), channel_id=1, source_target_pairs={{0,2},{1,3},{2,0},{3,1},{4,6},{5,7},{6,4},{7,5},{8,10},{9,11},{10,... | collective-permute-start | bytes 786440 | tf_op jit(solution)/shard_map/ppermute | solution.py:75
  51.2 4.0 %collective-permute-start.2 = (bf16[256,512]{0,1:T(8,128)(2,1)S(1)}, bf16[256,512]{0,1:T(8,128)(2,1)S(1)}, u32[]{:S(2)}, u32[]{:S(2)}) collective-permute-start(bf16[256,512]{0,1:T(8,128)(2,1)S(1)} %bitcast.109), channel_id=1, source_target_pairs={{0,3},{1,0},{2,1},{3,2},{4,7},{5,4},{6,5},{7,6},{8,11},{9,8},{10,9... | collective-permute-start | bytes 786440 | tf_op jit(solution)/shard_map/ppermute | solution.py:75
  55.2 2.4 %collective-permute-done.1 = bf16[256,512]{0,1:T(8,128)(2,1)S(1)} collective-permute-done((bf16[256,512]{0,1:T(8,128)(2,1)S(1)}, bf16[256,512]{0,1:T(8,128)(2,1)S(1)}, u32[]{:S(2)}, u32[]{:S(2)}) %collective-permute-start.1) | collective-permute-done | bytes 262176 | tf_op jit(solution)/shard_map/ppermute | solution.py:75
  57.6 4.6 %collective-permute-done.2 = bf16[256,512]{0,1:T(8,128)(2,1)S(1)} collective-permute-done((bf16[256,512]{0,1:T(8,128)(2,1)S(1)}, bf16[256,512]{0,1:T(8,128)(2,1)S(1)}, u32[]{:S(2)}, u32[]{:S(2)}) %collective-permute-start.2) | collective-permute-done | bytes 262176 | tf_op jit(solution)/shard_map/ppermute | solution.py:75
  62.1 1.1 pad_maximum_fusion
  63.3 1.9 gather_fusion.1
  65.1 0.2 broadcast_select_fusion.1
  65.5 35.2 %all-gather.2.cloned.1.call-done = bf16[1024,2816]{1,0:T(8,128)(2,1)} async-done(((bf16[64,2816]{1,0:T(8,128)(2,1)}), bf16[1024,2816]{1,0:T(8,128)(2,1)}) %all-gather.2.cloned.1.call-update) | async-done | bytes 5767184 | tf_op jit(solution)/shard_map/all_gather | solution.py:122
  100.7 7.7 %collective-permute-start.3 = (bf16[1024,2816]{1,0:T(8,128)(2,1)}, bf16[1024,2816]{1,0:T(8,128)(2,1)}, u32[]{:S(2)}, u32[]{:S(2)}) collective-permute-start(bf16[1024,2816]{1,0:T(8,128)(2,1)} %all-gather.2.cloned.1.call-done), channel_id=1, source_target_pairs={{0,4},{4,0},{1,5},{5,1},{2,6},{6,2},{3,7},{7,3},{8,12},{12,8},{9,1... | collective-permute-start | bytes 17301512 | tf_op jit(solution)/shard_map/ppermute | solution.py:126
  108.4 0.4 fusion.27
  109.0 1.7 fusion.31
  110.7 7.0 %collective-permute-done.3 = bf16[1024,2816]{1,0:T(8,128)(2,1)} collective-permute-done((bf16[1024,2816]{1,0:T(8,128)(2,1)}, bf16[1024,2816]{1,0:T(8,128)(2,1)}, u32[]{:S(2)}, u32[]{:S(2)}) %collective-permute-start.3) | collective-permute-done | bytes 5767200 | tf_op jit(solution)/shard_map/ppermute | solution.py:126
  117.8 1.7 fusion.26
  119.4 3.2 %collective-permute-start.4 = (bf16[256,512]{1,0:T(8,128)(2,1)S(1)}, bf16[256,512]{1,0:T(8,128)(2,1)S(1)}, u32[]{:S(2)}, u32[]{:S(2)}) collective-permute-start(bf16[256,512]{1,0:T(8,128)(2,1)S(1)} %fusion.26), channel_id=1, source_target_pairs={{0,1},{1,2},{2,3},{3,0},{4,5},{5,6},{6,7},{7,4},{8,9},{9,10},{10,1... | collective-permute-start | bytes 786440 | tf_op jit(solution)/shard_map/ppermute | solution.py:75
  122.7 2.7 %collective-permute-start.5 = (bf16[256,512]{1,0:T(8,128)(2,1)S(1)}, bf16[256,512]{1,0:T(8,128)(2,1)S(1)}, u32[]{:S(2)}, u32[]{:S(2)}) collective-permute-start(bf16[256,512]{1,0:T(8,128)(2,1)S(1)} %fusion.26), channel_id=1, source_target_pairs={{0,2},{1,3},{2,0},{3,1},{4,6},{5,7},{6,4},{7,5},{8,10},{9,11},{10,... | collective-permute-start | bytes 786440 | tf_op jit(solution)/shard_map/ppermute | solution.py:75
  125.4 3.4 %collective-permute-start.6 = (bf16[256,512]{1,0:T(8,128)(2,1)S(1)}, bf16[256,512]{1,0:T(8,128)(2,1)S(1)}, u32[]{:S(2)}, u32[]{:S(2)}) collective-permute-start(bf16[256,512]{1,0:T(8,128)(2,1)S(1)} %fusion.26), channel_id=1, source_target_pairs={{0,3},{1,0},{2,1},{3,2},{4,7},{5,4},{6,5},{7,6},{8,11},{9,8},{10,9... | collective-permute-start | bytes 786440 | tf_op jit(solution)/shard_map/ppermute | solution.py:75
  129.1 4.2 %collective-permute-done.5 = bf16[256,512]{1,0:T(8,128)(2,1)S(1)} collective-permute-done((bf16[256,512]{1,0:T(8,128)(2,1)S(1)}, bf16[256,512]{1,0:T(8,128)(2,1)S(1)}, u32[]{:S(2)}, u32[]{:S(2)}) %collective-permute-start.5) | collective-permute-done | bytes 262176 | tf_op jit(solution)/shard_map/ppermute | solution.py:75
  133.3 6.6 %collective-permute-done.6 = bf16[256,512]{1,0:T(8,128)(2,1)S(1)} collective-permute-done((bf16[256,512]{1,0:T(8,128)(2,1)S(1)}, bf16[256,512]{1,0:T(8,128)(2,1)S(1)}, u32[]{:S(2)}, u32[]{:S(2)}) %collective-permute-start.6) | collective-permute-done | bytes 262176 | tf_op jit(solution)/shard_map/ppermute | solution.py:75
  139.9 1.1 pad_maximum_fusion.2
  141.0 1.8 gather_fusion.2
  142.9 0.2 broadcast_select_fusion
  143.1 0.1 slice_bitcast_fusion.7
  143.2 0.3 multiply_reduce_fusion
  143.5 0.1 copy.56
  143.6 0.1 copy.57
  143.8 0.1 copy.58
  144.1 0.3 multiply_convert_fusion
  144.4 0.5 fusion.28
  145.0 2.9 %fusion.4 = f32[256,1536]{1,0:T(8,128)S(1)} fusion(bf16[1024,2816]{1,0:T(8,128)(2,1)} %all-gather.2.cloned.1.call-done, bf16[256,2048]{0,1:T(8,128)(2,1)S(1)} %bitcast.96), kind=kOutput, calls=%fused_computation.7 | convolution fusion | flops 805306368 | bytes 5242880 | tf_op jit(solution)/shard_map/dot_general | solution.py:133
  147.9 2.9 %fusion.6 = f32[256,1536]{1,0:T(8,128)S(1)} fusion(f32[256,1536]{1,0:T(8,128)S(1)} %fusion.4, bf16[1024,2816]{1,0:T(8,128)(2,1)} %collective-permute-done.3, bf16[256,2048]{0,1:T(8,128)(2,1)S(1)} %bitcast.97), kind=kOutput, calls=%fused_computation.9 | convolution fusion | flops 805699584 | bytes 6815744 | tf_op jit(solution)/shard_map/dot_general | solution.py:133
  150.8 0.2 fusion.41
  151.0 0.7 copy-done.3
  151.8 2.0 %fusion.15 = bf16[256,1024]{1,0:T(8,128)(2,1)S(1)} fusion(bf16[256,768]{1,0:T(8,128)(2,1)S(1)} %fusion.41, bf16[1024,2816]{1,0:T(8,128)(2,1)} %all-gather.2.cloned.1.call-done), kind=kOutput, calls=%fused_computation.29 | convolution fusion | flops 402915328 | bytes 2490368 | tf_op jit(solution)/shard_map/dot_general | solution.py:90
  153.8 0.2 copy.61
  154.0 2.1 %fusion.18 = bf16[256,1024]{1,0:T(8,128)(2,1)S(1)} fusion(bf16[256,768]{1,0:T(8,128)(2,1)} %copy-done.3, bf16[1024,2816]{1,0:T(8,128)(2,1)} %collective-permute-done.3), kind=kOutput, calls=%fused_computation.30 | convolution fusion | flops 402915328 | bytes 2490368 | tf_op jit(solution)/shard_map/dot_general | solution.py:90
  156.2 0.2 copy.62
  156.5 0.8 copy.63
  157.4 1.9 %collective-permute-start.7 = (bf16[256,512]{1,0:T(8,128)(2,1)}, bf16[256,512]{1,0:T(8,128)(2,1)}, u32[]{:S(2)}, u32[]{:S(2)}) collective-permute-start(bf16[256,512]{1,0:T(8,128)(2,1)} %copy.63), channel_id=1, source_target_pairs={{0,1},{1,2},{2,3},{3,0},{4,5},{5,6},{6,7},{7,4},{8,9},{9,10},{10,1... | collective-permute-start | bytes 786440 | tf_op jit(solution)/shard_map/ppermute | solution.py:105
  159.3 0.8 copy.65
  160.2 2.5 %collective-permute-start.8 = (bf16[256,512]{1,0:T(8,128)(2,1)}, bf16[256,512]{1,0:T(8,128)(2,1)S(1)}, u32[]{:S(2)}, u32[]{:S(2)}) collective-permute-start(bf16[256,512]{1,0:T(8,128)(2,1)} %copy.65), channel_id=1, source_target_pairs={{0,2},{1,3},{2,0},{3,1},{4,6},{5,7},{6,4},{7,5},{8,10},{9,11},{10,... | collective-permute-start | bytes 786440 | tf_op jit(solution)/shard_map/ppermute | solution.py:105
  162.7 0.8 copy.66
  163.5 4.0 %collective-permute-start.9 = (bf16[256,512]{1,0:T(8,128)(2,1)}, bf16[256,512]{1,0:T(8,128)(2,1)S(1)}, u32[]{:S(2)}, u32[]{:S(2)}) collective-permute-start(bf16[256,512]{1,0:T(8,128)(2,1)} %copy.66), channel_id=1, source_target_pairs={{0,3},{1,0},{2,1},{3,2},{4,7},{5,4},{6,5},{7,6},{8,11},{9,8},{10,9... | collective-permute-start | bytes 786440 | tf_op jit(solution)/shard_map/ppermute | solution.py:105
  167.6 0.2 copy.64
  167.8 2.7 %collective-permute-done.8 = bf16[256,512]{1,0:T(8,128)(2,1)S(1)} collective-permute-done((bf16[256,512]{1,0:T(8,128)(2,1)}, bf16[256,512]{1,0:T(8,128)(2,1)S(1)}, u32[]{:S(2)}, u32[]{:S(2)}) %collective-permute-start.8) | collective-permute-done | bytes 262176 | tf_op jit(solution)/shard_map/ppermute | solution.py:105
  170.5 7.1 %collective-permute-done.9 = bf16[256,512]{1,0:T(8,128)(2,1)S(1)} collective-permute-done((bf16[256,512]{1,0:T(8,128)(2,1)}, bf16[256,512]{1,0:T(8,128)(2,1)S(1)}, u32[]{:S(2)}, u32[]{:S(2)}) %collective-permute-start.9) | collective-permute-done | bytes 262176 | tf_op jit(solution)/shard_map/ppermute | solution.py:105
  177.6 1.8 add_convert_fusion
  (45 shorter events, 1.2 us)
Async XLA Ops:
  6.5 10.8 %copy-start = (bf16[6,128,2,512]{3,2,1,0:T(2,128)(2,1)S(1)}, bf16[6,128,2,512]{3,2,1,0:T(2,128)(2,1)}, u32[]{:S(2)}) copy-start(bf16[6,128,2,512]{3,2,1,0:T(2,128)(2,1)} %param.18) | copy-start | bytes 4718596
  6.5 94.1 %all-gather.2.cloned.1.call-start = ((), (), s32[]{:S(2)}) async-start(), calls=%async_computation.1 | async-start | bytes 6127616 | tf_op jit(solution)/shard_map/all_gather | solution.py:122
  22.9 1.8 copy-start.2
  22.9 3.3 %copy-start.5 = (f32[4,128]{1,0:T(4,128)S(1)}, f32[4,128]{1,0:T(4,128)}, u32[]{:S(2)}) copy-start(f32[4,128]{1,0:T(4,128)} %param.22) | copy-start | bytes 6148
  22.9 5.3 %copy-start.8 = (s32[128]{0:T(128)S(1)}, s32[128]{0:T(128)}, u32[]{:S(2)}) copy-start(s32[128]{0:T(128)} %param.21) | copy-start | bytes 1540
  22.9 6.8 %copy-start.9 = (s32[1,6]{1,0:T(1,128)S(1)}, s32[1,6]{1,0:T(1,128)}, u32[]{:S(2)}) copy-start(s32[1,6]{1,0:T(1,128)} %param.19) | copy-start | bytes 76
  33.3 2.3 %copy-start.1 = (bf16[768,2,512]{2,0,1:T(8,128)(2,1)S(1)}, bf16[768,2,512]{2,0,1:T(8,128)(2,1)}, u32[]{:S(2)}) copy-start(bf16[768,2,512]{2,0,1:T(8,128)(2,1)} %bitcast_select_fusion.4) | copy-start | bytes 4718596
  40.8 3.4 %copy-start.6 = (f32[256]{0:T(256)S(1)}, f32[256]{0:T(256)}, u32[]{:S(2)}) copy-start(f32[256]{0:T(256)} %param.23) | copy-start | bytes 3076
  45.3 9.9 %collective-permute-start = (bf16[256,512]{0,1:T(8,128)(2,1)S(1)}, bf16[256,512]{0,1:T(8,128)(2,1)S(1)}, u32[]{:S(2)}, u32[]{:S(2)}) collective-permute-start(bf16[256,512]{0,1:T(8,128)(2,1)S(1)} %bitcast.107), channel_id=1, source_target_pairs={{0,1},{1,2},{2,3},{3,0},{4,5},{5,6},{6,7},{7,4},{8,9},{9,10},{10,1... | collective-permute-start | bytes 786440 | tf_op jit(solution)/shard_map/ppermute | solution.py:75
  48.5 9.0 %collective-permute-start.1 = (bf16[256,512]{0,1:T(8,128)(2,1)S(1)}, bf16[256,512]{0,1:T(8,128)(2,1)S(1)}, u32[]{:S(2)}, u32[]{:S(2)}) collective-permute-start(bf16[256,512]{0,1:T(8,128)(2,1)S(1)} %bitcast.108), channel_id=1, source_target_pairs={{0,2},{1,3},{2,0},{3,1},{4,6},{5,7},{6,4},{7,5},{8,10},{9,11},{10,... | collective-permute-start | bytes 786440 | tf_op jit(solution)/shard_map/ppermute | solution.py:75
  51.2 11.0 %collective-permute-start.2 = (bf16[256,512]{0,1:T(8,128)(2,1)S(1)}, bf16[256,512]{0,1:T(8,128)(2,1)S(1)}, u32[]{:S(2)}, u32[]{:S(2)}) collective-permute-start(bf16[256,512]{0,1:T(8,128)(2,1)S(1)} %bitcast.109), channel_id=1, source_target_pairs={{0,3},{1,0},{2,1},{3,2},{4,7},{5,4},{6,5},{7,6},{8,11},{9,8},{10,9... | collective-permute-start | bytes 786440 | tf_op jit(solution)/shard_map/ppermute | solution.py:75
  100.7 17.1 %collective-permute-start.3 = (bf16[1024,2816]{1,0:T(8,128)(2,1)}, bf16[1024,2816]{1,0:T(8,128)(2,1)}, u32[]{:S(2)}, u32[]{:S(2)}) collective-permute-start(bf16[1024,2816]{1,0:T(8,128)(2,1)} %all-gather.2.cloned.1.call-done), channel_id=1, source_target_pairs={{0,4},{4,0},{1,5},{5,1},{2,6},{6,2},{3,7},{7,3},{8,12},{12,8},{9,1... | collective-permute-start | bytes 17301512 | tf_op jit(solution)/shard_map/ppermute | solution.py:126
  108.9 8.9 %copy-start.7 = (bf16[256,512]{1,0:T(8,128)(2,1)S(1)}, bf16[256,512]{1,0:T(8,128)(2,1)}, u32[]{:S(2)}) copy-start(bf16[256,512]{1,0:T(8,128)(2,1)} %param.24) | copy-start | bytes 786436
  110.7 18.2 %copy-start.4 = (f32[2048]{0:T(1024)S(1)}, f32[2048]{0:T(1024)}, u32[]{:S(2)}) copy-start(f32[2048]{0:T(1024)} %param.26) | copy-start | bytes 24580
  119.4 9.6 %collective-permute-start.4 = (bf16[256,512]{1,0:T(8,128)(2,1)S(1)}, bf16[256,512]{1,0:T(8,128)(2,1)S(1)}, u32[]{:S(2)}, u32[]{:S(2)}) collective-permute-start(bf16[256,512]{1,0:T(8,128)(2,1)S(1)} %fusion.26), channel_id=1, source_target_pairs={{0,1},{1,2},{2,3},{3,0},{4,5},{5,6},{6,7},{7,4},{8,9},{9,10},{10,1... | collective-permute-start | bytes 786440 | tf_op jit(solution)/shard_map/ppermute | solution.py:75
  122.7 10.6 %collective-permute-start.5 = (bf16[256,512]{1,0:T(8,128)(2,1)S(1)}, bf16[256,512]{1,0:T(8,128)(2,1)S(1)}, u32[]{:S(2)}, u32[]{:S(2)}) collective-permute-start(bf16[256,512]{1,0:T(8,128)(2,1)S(1)} %fusion.26), channel_id=1, source_target_pairs={{0,2},{1,3},{2,0},{3,1},{4,6},{5,7},{6,4},{7,5},{8,10},{9,11},{10,... | collective-permute-start | bytes 786440 | tf_op jit(solution)/shard_map/ppermute | solution.py:75
  125.4 14.5 %collective-permute-start.6 = (bf16[256,512]{1,0:T(8,128)(2,1)S(1)}, bf16[256,512]{1,0:T(8,128)(2,1)S(1)}, u32[]{:S(2)}, u32[]{:S(2)}) collective-permute-start(bf16[256,512]{1,0:T(8,128)(2,1)S(1)} %fusion.26), channel_id=1, source_target_pairs={{0,3},{1,0},{2,1},{3,2},{4,7},{5,4},{6,5},{7,6},{8,11},{9,8},{10,9... | collective-permute-start | bytes 786440 | tf_op jit(solution)/shard_map/ppermute | solution.py:75
  151.0 0.8 copy-start.3
  157.4 10.4 %collective-permute-start.7 = (bf16[256,512]{1,0:T(8,128)(2,1)}, bf16[256,512]{1,0:T(8,128)(2,1)}, u32[]{:S(2)}, u32[]{:S(2)}) collective-permute-start(bf16[256,512]{1,0:T(8,128)(2,1)} %copy.63), channel_id=1, source_target_pairs={{0,1},{1,2},{2,3},{3,0},{4,5},{5,6},{6,7},{7,4},{8,9},{9,10},{10,1... | collective-permute-start | bytes 786440 | tf_op jit(solution)/shard_map/ppermute | solution.py:105
  160.2 10.3 %collective-permute-start.8 = (bf16[256,512]{1,0:T(8,128)(2,1)}, bf16[256,512]{1,0:T(8,128)(2,1)S(1)}, u32[]{:S(2)}, u32[]{:S(2)}) collective-permute-start(bf16[256,512]{1,0:T(8,128)(2,1)} %copy.65), channel_id=1, source_target_pairs={{0,2},{1,3},{2,0},{3,1},{4,6},{5,7},{6,4},{7,5},{8,10},{9,11},{10,... | collective-permute-start | bytes 786440 | tf_op jit(solution)/shard_map/ppermute | solution.py:105
  163.5 14.1 %collective-permute-start.9 = (bf16[256,512]{1,0:T(8,128)(2,1)}, bf16[256,512]{1,0:T(8,128)(2,1)S(1)}, u32[]{:S(2)}, u32[]{:S(2)}) collective-permute-start(bf16[256,512]{1,0:T(8,128)(2,1)} %copy.66), channel_id=1, source_target_pairs={{0,3},{1,0},{2,1},{3,2},{4,7},{5,4},{6,5},{7,6},{8,11},{9,8},{10,9... | collective-permute-start | bytes 786440 | tf_op jit(solution)/shard_map/ppermute | solution.py:105
Sparse Core Ops, SparseCore 0:
  16.8 83.8 all-gather.1
